TPU v7x, 32 devices: a whole 2x2x4 slice. The times are simulated.
32 devices in a mesh: groups: 2 (over y), events: 8 (over z, x), heads: 2 (over core).
Axes of the slice: x: 2, y: 2, z: 4, core: 2. Of those that a mesh axis runs over, the one named last changes fastest.
Arguments:
- inputs: bfloat16 [256, 1024], P(('groups', 'events')), parts along dimension 0, may hold values from -6 to 6
- cand_user: int32 [256], P('groups'), parts along dimension 0, may hold values from 0 to 3, as said below
- event_user: int32 [8192], P(('groups', 'events')), parts along dimension 0, may hold values from 0 to 3, as said below
- event_count: int32 [16], P(('groups', 'events')), parts along dimension 0, may hold values from 128 to 512, as said below
- w_qu: bfloat16 [1024, 2, 1024], P(None, None, 'heads'), may hold values from -0.1875 to 0.1875
- keys: bfloat16 [8192, 1024], P(('groups', 'events'), 'heads'), parts along dimension 0, may hold values from -6 to 6
- values: bfloat16 [8192, 1024], P(('groups', 'events'), 'heads'), parts along dimension 0, may hold values from -6 to 6
- gain: float32 [1024], P('heads'), may hold values from 0.1 to 1.9
- w_out: bfloat16 [1024, 1024], P('heads'), may hold values from -0.1875 to 0.1875
Outputs:
- scored: bfloat16 [256, 1024], P(('groups', 'events')), parts along dimension 0
There are 2 independent parts, one for each index of `groups`. A program takes and returns all parts, laid end to end along the dimension named above; an argument that names none is the same for every part. Nothing has to cross between parts.
Inputs may be any that keep to these rules, and one draw needn't show every extreme that they name: `event_count`: each cache shard's filled slots come first; some shard is full and some holds 128. `event_user`: Users' events are consecutive and in increasing user order over the whole cache; every user has 1 to 2047 events, and some user has exactly 2047. `cand_user`: every candidate belongs to a user that has at least one filled slot somewhere in the cache.
All inputs are finite; a program needn't handle non-finite values.
Results may differ from a plain program's by a relative error of at most 0.0075.
Values may be sent and summed in bfloat16 or wider, within the bound.
No kernel may reach another device: no remote copies, remote signals or barrier semaphores. Data moves between devices by JAX's collectives and lax.ppermute only.
A program may use at most 64 MiB of HBM per device.

v0:
```python
import math
import jax
import jax.numpy as jnp
from jax import lax
from jax.sharding import PartitionSpec as P

DH = 128
HD = 1024
epsilon = 1e-05


def shards(inputs, cand_user, event_user, event_count, w_qu, keys, values, gain, w_out):
    row_count = inputs.shape[0]
    feat_width = inputs.shape[1]
    local_width = w_qu.shape[2]
    heads_here = local_width // DH
    slot_total = keys.shape[0]
    score_scale = 1.0 / math.sqrt(DH)
    packed_weight = w_qu.reshape(feat_width, 2 * local_width)
    query_weight = packed_weight[:, :local_width]
    gate_weight = packed_weight[:, local_width:]
    gate_values = jax.nn.silu(
        jnp.dot(inputs, gate_weight, preferred_element_type=jnp.float32)
    ).astype(jnp.bfloat16)
    gathered_rows = lax.all_gather(inputs, "events", axis=0, tiled=True)
    queries = jax.nn.silu(
        jnp.dot(gathered_rows, query_weight, preferred_element_type=jnp.float32)
    ).astype(jnp.bfloat16)
    slot_index = jnp.arange(slot_total, dtype=jnp.int32)
    slot_valid = slot_index < event_count[0]
    key_heads = keys.reshape(slot_total, heads_here, DH)
    value_heads = values.reshape(slot_total, heads_here, DH)

    def attend_rows(query_rows, row_users):
        rows_here = query_rows.shape[0]
        query_block = query_rows.reshape(rows_here, heads_here, DH)
        user_match = ((row_users[:, None] == event_user[None, :]) & slot_valid[None, :]).astype(
            jnp.float32
        )
        scores = (
            jnp.einsum("chd,ehd->hce", query_block, key_heads, preferred_element_type=jnp.float32)
            * score_scale
        )
        attn_weights = (jax.nn.silu(scores) * user_match[None]).astype(jnp.bfloat16)
        partial_out = jnp.einsum(
            "hce,ehd->chd", attn_weights, value_heads, preferred_element_type=jnp.float32
        )
        return partial_out.reshape(rows_here, local_width)

    block_rows = math.gcd(row_count * lax.axis_size("events"), 512)
    block_count = row_count * lax.axis_size("events") // block_rows

    def compute_block(which_block):
        block_start = which_block * block_rows
        query_rows = lax.dynamic_slice_in_dim(queries, block_start, block_rows, 0)
        block_users = lax.dynamic_slice_in_dim(cand_user, block_start, block_rows, 0)
        return attend_rows(query_rows, block_users)

    stacked = lax.map(compute_block, jnp.arange(block_count, dtype=jnp.int32))
    attended = lax.psum_scatter(
        stacked.reshape(row_count * lax.axis_size("events"), local_width),
        "events",
        scatter_dimension=0,
        tiled=True,
    )
    first_moment = jnp.sum(attended, axis=1)
    second_moment = jnp.sum(attended * attended, axis=1)
    total_first, total_second = lax.psum((first_moment, second_moment), "heads")
    average = total_first / HD
    variance = total_second / HD - average * average
    normed = (attended - average[:, None]) * lax.rsqrt(variance + epsilon)[:, None] * gain
    gated = (normed * gate_values.astype(jnp.float32)).astype(jnp.bfloat16)
    projected = jnp.dot(gated, w_out, preferred_element_type=jnp.float32)
    summed_heads = lax.psum(projected, "heads")
    return (inputs.astype(jnp.float32) + summed_heads).astype(jnp.bfloat16)


def solution(mesh):
    placed = (
        P(("groups", "events"), None),
        P("groups"),
        P(("groups", "events")),
        P(("groups", "events")),
        P(None, None, "heads"),
        P(("groups", "events"), "heads"),
        P(("groups", "events"), "heads"),
        P("heads"),
        P("heads", None),
    )
    return jax.shard_map(
        shards, mesh=mesh, in_specs=placed, out_specs=P(("groups", "events"), None), check_vma=False
    )
```

profile of v0, /device:TPU:0, one launch (start us, length us, event | category | flops | bytes accessed | tf_op | source)
XLA Modules:
  0.0 143.9 jit_solution(11439747766623471906)
XLA Ops:
  6.5 0.0 copy-start
  6.5 0.0 reduce-scatter.2.cloned.1.call-start
  7.3 32.8 %all_gather.3 = bf16[128,1024]{1,0:T(8,128)(2,1)S(1)} all-gather(bf16[16,1024]{1,0:T(8,128)(2,1)} %param.9), channel_id=1, replica_groups=mesh['groups'=2,'events'=8,'heads'=2] {'events'}, dimensions={0}, use_global_device_ids=true | all-gather | bytes 294912 | tf_op jit(solution)/shard_map/all_gather | solution.py:25
  40.1 2.0 %copy.14 = bf16[512,512]{0,1:T(8,128)(2,1)} copy(bf16[512,512]{1,0:T(8,128)(2,1)} %param.15) | data formatting | bytes 1048576 | tf_op jit(solution)/shard_map/reshape | solution.py:32
  42.1 2.2 %copy.17 = bf16[128,8,2,512]{3,1,2,0:T(8,128)(2,1)S(1)} copy(bf16[128,8,2,512]{3,2,1,0:T(2,128)(2,1)} %bitcast.29) | data formatting | bytes 4194304
  44.3 0.0 copy-start.4
  44.3 1.0 fusion.14
  45.3 0.0 copy-done.2
  45.3 0.0 copy-done.4
  45.3 0.1 and_convert_fusion
  45.4 0.0 copy-start.1
  45.4 0.0 copy-start.3
  45.4 2.6 %fusion.4 = f32[4,128,128]{1,2,0:T(8,128)} fusion(bf16[512,4,128]{0,2,1:T(8,128)(2,1)} %bitcast.30, f32[128,512]{1,0:T(8,128)S(1)} %and_convert_fusion, bf16[16,4,8,128]{3,2,1,0:T(8,128)(2,1)} %fusion.14, bf16[512,512]{1,0:T(8,128)(2,1)} %param.14), kind=kOutput, calls=%fused_computation.6 | convolution fusion | flops 136052736 | bytes 1703936 | tf_op jit(solution)/shard_map/while/body/eval_jaxpr/hce,ehd->chd/dot_general | solution.py:45
  48.1 1.8 %copy.13 = f32[128,512]{1,0:T(8,128)} copy(f32[128,512]{0,1:T(8,128)} %bitcast.31) | data formatting | bytes 524288 | tf_op jit(solution)/shard_map/reshape | solution.py:61
  49.9 0.0 reduce-scatter.2.cloned.1.call-update
  49.9 0.0 all-reduce.3.cloned.1.call-start
  49.9 63.5 %reduce-scatter.2.cloned.1.call-done = f32[16,512]{1,0:T(8,128)} async-done(((f32[128,512]{1,0:T(8,128)}), f32[16,512]{1,0:T(8,128)}) %reduce-scatter.2.cloned.1.call-update) | async-done | bytes 32784 | tf_op jit(solution)/shard_map/reduce_scatter | solution.py:60
  113.5 0.9 fusion.38
  114.3 2.5 %all-reduce = (f32[16]{0:T(128)S(1)}, f32[16]{0:T(128)S(1)}) all-reduce(f32[16]{0:T(128)S(1)} %get-tuple-element.20, f32[16]{0:T(128)S(1)} %get-tuple-element.19), channel_id=1, replica_groups=mesh['groups'=2,'events'=8,'heads'=2] {'heads'}, use_global_device_ids=true, to_apply=%region_4.5 | all-reduce | flops 32 | bytes 256 | tf_op jit(solution)/shard_map/psum | solution.py:68
  116.8 0.0 copy-done
  116.8 1.9 %fusion.26 = f32[16,1024]{1,0:T(8,128)} fusion(bf16[512,1024]{1,0:T(8,128)(2,1)S(1)} %copy-done, bf16[16,1024]{1,0:T(8,128)(2,1)S(1)} %copy-done.1, bf16[1024,1024]{1,0:T(8,128)(2,1)S(1)} %bitcast.28, f32[16,512]{1,0:T(8,128)} %reduce-scatter.2.cloned.1.call-done, f32[512]{0:T(512)S(1)} %copy-done.3, f32[16]{0:T(128)S(1)} %get-tuple-element.32, ...), kind=kOutput, calls=%fused_computation.20 | convolution fusion | flops 33644544 | bytes 2231296 | tf_op jit(solution)/shard_map/dot_general | solution.py:73
  118.7 0.0 all-reduce.3.cloned.1.call-update
  118.7 16.9 %all-reduce.3.cloned.1.call-done = f32[16,1024]{1,0:T(8,128)} async-done(((f32[16,1024]{1,0:T(8,128)}), f32[16,1024]{1,0:T(8,128)}) %all-reduce.3.cloned.1.call-update) | async-done | bytes 65552 | tf_op jit(solution)/shard_map/psum | solution.py:74
  135.6 1.5 %add_convert_fusion = bf16[16,1024]{1,0:T(8,128)(2,1)} fusion(f32[16,1024]{1,0:T(8,128)} %all-reduce.3.cloned.1.call-done, bf16[16,1024]{1,0:T(8,128)(2,1)S(1)} %copy-done.1), kind=kLoop, calls=%fused_computation.17 | loop fusion | flops 49152 | bytes 131072 | tf_op jit(solution)/shard_map/convert_element_type | solution.py:75
  (5 shorter events, 0.0 us)
Async XLA Ops:
  6.5 110.3 %copy-start = (bf16[512,1024]{1,0:T(8,128)(2,1)S(1)}, bf16[512,1024]{1,0:T(8,128)(2,1)}, u32[]{:S(2)}) copy-start(bf16[512,1024]{1,0:T(8,128)(2,1)} %param.17) | copy-start | bytes 3145732
  6.5 106.9 %reduce-scatter.2.cloned.1.call-start = ((), (), s32[]{:S(2)}) async-start(), calls=%async_computation.1 | async-start | bytes 294912 | tf_op jit(solution)/shard_map/reduce_scatter | solution.py:60
  44.3 1.0 copy-start.2
  44.3 1.0 copy-start.4
  45.4 71.4 %copy-start.1 = (bf16[16,1024]{1,0:T(8,128)(2,1)S(1)}, bf16[16,1024]{1,0:T(8,128)(2,1)}, u32[]{:S(2)}) copy-start(bf16[16,1024]{1,0:T(8,128)(2,1)} %param.9) | copy-start | bytes 98308
  45.4 71.4 %copy-start.3 = (f32[512]{0:T(512)S(1)}, f32[512]{0:T(512)}, u32[]{:S(2)}) copy-start(f32[512]{0:T(512)} %param.16) | copy-start | bytes 6148
  49.9 85.7 %all-reduce.3.cloned.1.call-start = ((), (), s32[]{:S(2)}) async-start(), calls=%async_computation.2 | async-start | bytes 131072 | tf_op jit(solution)/shard_map/psum | solution.py:74
Sparse Core Ops, SparseCore 0:
  50.0 63.4 reduce-scatter.1
  118.8 16.7 all-reduce.2
where the time goes:
time: 144 us
  waiting for transfers between devices  80.5 us (56%)
  blocking collectives  35.2 us (24%)
  between operations  14.2 us (10%)
  local copies, waits for them, and re-layouts  6 us (4%)
  matrix products  5.52 us (4%)
  other arithmetic  2.45 us (2%)
    reduce_scatter x1, waiting for transfers between devices, shards(): lax.psum_scatter(stacked.reshape(row_count * lax.axis_size('events'), loc...  63.5 us
    all_gather x1, blocking collectives, shards(): gathered_rows = lax.all_gather(inputs, 'events', axis=0, tiled=True)  32.8 us
    psum x1, waiting for transfers between devices, shards(): summed_heads = lax.psum(projected, 'heads')  16.9 us
  transfers between devices with their start and end apart: 2, of which 2 were waited for; matrix products, arithmetic and copies ran while one was open for 0% of the time, Pallas kernels for 0%

commit v1 on v0

--- a/solution.py
+++ b/solution.py
@@ -7,6 +7,25 @@
 DH = 128
 HD = 1024
 epsilon = 1e-05
+
+
+def in_order(pieces, dim):
+    pieces = jnp.moveaxis(pieces, 0, dim)
+    lengths = pieces.shape
+    return pieces.reshape(*lengths[:dim], lengths[dim] * lengths[dim + 1], *lengths[dim + 2 :])
+
+
+def grow_blocks(shard, axis):
+    size, mine = (lax.axis_size(axis), lax.axis_index(axis))
+    blocks, bit = (shard[None], 1)
+    while bit < size:
+        received = lax.ppermute(blocks, axis, [(i, i ^ bit) for i in range(size)])
+        low = mine & bit == 0
+        blocks = jnp.concatenate(
+            [jnp.where(low, blocks, received), jnp.where(low, received, blocks)]
+        )
+        bit *= 2
+    return blocks
 
 
 def shards(inputs, cand_user, event_user, event_count, w_qu, keys, values, gain, w_out):
@@ -22,7 +41,7 @@
     gate_values = jax.nn.silu(
         jnp.dot(inputs, gate_weight, preferred_element_type=jnp.float32)
     ).astype(jnp.bfloat16)
-    gathered_rows = lax.all_gather(inputs, "events", axis=0, tiled=True)
+    gathered_rows = in_order(grow_blocks(inputs, "events"), 0)
     queries = jax.nn.silu(
         jnp.dot(gathered_rows, query_weight, preferred_element_type=jnp.float32)
     ).astype(jnp.bfloat16)

time: 144 us -> 125 us (0.87)
  blocking collectives: 35.2 us -> 2.46 us
  starting transfers between devices: 0.04 us -> 7.31 us
  waiting for transfers between devices: 80.5 us -> 86.9 us
    all_gather x1 -> x0, blocking collectives: 32.8 us -> none  [shards(): gathered_rows = lax.all_gather(inputs, 'events', axis=0, tiled=True)]
    ppermute x0 -> x3, waiting for transfers between devices: none -> 7.49 us  [grow_blocks(): received = lax.ppermute(blocks, axis, [(i, i ^ bit) for i in range(size)])]
    ppermute x0 -> x3, starting transfers between devices: none -> 7.26 us  [grow_blocks(): received = lax.ppermute(blocks, axis, [(i, i ^ bit) for i in range(size)])]
  transfers between devices with their start and end apart: 2 -> 5, of which waited for: 2 -> 4; matrix products, arithmetic and copies ran while one was open for 0% -> 3% of each run, Pallas kernels for 0% -> 0%
where the time goes in v1:
time: 125 us
  waiting for transfers between devices  86.9 us (70%)
  between operations  14.1 us (11%)
  starting transfers between devices  7.31 us (6%)
  local copies, waits for them, and re-layouts  6 us (5%)
  matrix products  5.53 us (4%)
  other arithmetic  2.55 us (2%)
  blocking collectives  2.46 us (2%)
    reduce_scatter x1, waiting for transfers between devices, shards(): lax.psum_scatter(stacked.reshape(row_count * lax.axis_size('events'), loc...  62.4 us
    psum x1, waiting for transfers between devices, shards(): summed_heads = lax.psum(projected, 'heads')  16.9 us
    ppermute x3, waiting for transfers between devices, grow_blocks(): received = lax.ppermute(blocks, axis, [(i, i ^ bit) for i in range(size)])  7.49 us
    ppermute x3, starting transfers between devices, grow_blocks(): received = lax.ppermute(blocks, axis, [(i, i ^ bit) for i in range(size)])  7.26 us
    dot_general x1, matrix products, attend_rows(): jnp.einsum('hce,ehd->chd', attn_weights, value_heads, preferred_element_t...  2.64 us
  transfers between devices with their start and end apart: 5, of which 4 were waited for; matrix products, arithmetic and copies ran while one was open for 3% of the time, Pallas kernels for 0%

profile of v1, /device:TPU:0, one launch (start us, length us, event | category | flops | bytes accessed | tf_op | source)
XLA Modules:
  0.0 124.9 jit_solution(10235194845936673603)
XLA Ops:
  6.5 0.0 copy-start
  6.5 0.0 reduce-scatter.2.cloned.1.call-start
  6.5 3.0 %collective-permute-start = (bf16[1,16,1024]{2,1,0:T(8,128)(2,1)}, bf16[1,16,1024]{2,1,0:T(8,128)(2,1)S(1)}, u32[]{:S(2)}, u32[]{:S(2)}) collective-permute-start(bf16[1,16,1024]{2,1,0:T(8,128)(2,1)} %bitcast.35), channel_id=1, source_target_pairs={{0,2},{2,0},{4,6},{6,4},{8,10},{10,8},{12,14},{14,12},{1,3},{3,1},... | collective-permute-start | bytes 98312 | tf_op jit(solution)/shard_map/ppermute | solution.py:22
  10.2 2.0 %copy.14 = bf16[512,512]{0,1:T(8,128)(2,1)} copy(bf16[512,512]{1,0:T(8,128)(2,1)} %param.15) | data formatting | bytes 1048576 | tf_op jit(solution)/shard_map/reshape | solution.py:51
  12.2 2.2 %copy.17 = bf16[128,8,2,512]{3,1,2,0:T(8,128)(2,1)S(1)} copy(bf16[128,8,2,512]{3,2,1,0:T(2,128)(2,1)} %bitcast.33) | data formatting | bytes 4194304
  14.4 0.0 collective-permute-done
  14.4 1.6 %collective-permute-start.1 = (bf16[2,16,1024]{2,1,0:T(8,128)(2,1)S(1)}, bf16[2,16,1024]{2,1,0:T(8,128)(2,1)S(1)}, u32[]{:S(2)}, u32[]{:S(2)}) collective-permute-start(bf16[2,16,1024]{2,1,0:T(8,128)(2,1)S(1)} %pad_maximum_fusion.2), channel_id=1, source_target_pairs={{0,4},{2,6},{4,0},{6,2},{8,12},{10,14},{12,8},{14,10},{1,5},{3,7},... | collective-permute-start | bytes 196616 | tf_op jit(solution)/shard_map/ppermute | solution.py:22
  16.1 2.7 %collective-permute-done.1 = bf16[2,16,1024]{2,1,0:T(8,128)(2,1)S(1)} collective-permute-done((bf16[2,16,1024]{2,1,0:T(8,128)(2,1)S(1)}, bf16[2,16,1024]{2,1,0:T(8,128)(2,1)S(1)}, u32[]{:S(2)}, u32[]{:S(2)}) %collective-permute-start.1) | collective-permute-done | bytes 65568 | tf_op jit(solution)/shard_map/ppermute | solution.py:22
  18.8 2.7 %collective-permute-start.2 = (bf16[4,16,1024]{2,1,0:T(8,128)(2,1)S(1)}, bf16[4,16,1024]{2,1,0:T(8,128)(2,1)S(1)}, u32[]{:S(2)}, u32[]{:S(2)}) collective-permute-start(bf16[4,16,1024]{2,1,0:T(8,128)(2,1)S(1)} %pad_maximum_fusion.1), channel_id=1, source_target_pairs={{0,8},{2,10},{4,12},{6,14},{8,0},{10,2},{12,4},{14,6},{1,9},{3,11}... | collective-permute-start | bytes 393224 | tf_op jit(solution)/shard_map/ppermute | solution.py:22
  21.5 0.1 and_convert_fusion
  21.6 4.8 %collective-permute-done.2 = bf16[4,16,1024]{2,1,0:T(8,128)(2,1)S(1)} collective-permute-done((bf16[4,16,1024]{2,1,0:T(8,128)(2,1)S(1)}, bf16[4,16,1024]{2,1,0:T(8,128)(2,1)S(1)}, u32[]{:S(2)}, u32[]{:S(2)}) %collective-permute-start.2) | collective-permute-done | bytes 131104 | tf_op jit(solution)/shard_map/ppermute | solution.py:22
  26.4 1.0 fusion.14
  27.5 2.6 %fusion.4 = f32[4,128,128]{1,2,0:T(8,128)} fusion(bf16[512,4,128]{0,2,1:T(8,128)(2,1)} %bitcast.34, f32[128,512]{1,0:T(8,128)S(1)} %and_convert_fusion, bf16[16,4,8,128]{3,2,1,0:T(8,128)(2,1)} %fusion.14, bf16[512,512]{1,0:T(8,128)(2,1)} %param.14), kind=kOutput, calls=%fused_computation.6 | convolution fusion | flops 136052736 | bytes 1703936 | tf_op jit(solution)/shard_map/while/body/eval_jaxpr/hce,ehd->chd/dot_general | solution.py:64
  30.1 1.8 %copy.13 = f32[128,512]{1,0:T(8,128)} copy(f32[128,512]{0,1:T(8,128)} %bitcast.36) | data formatting | bytes 524288 | tf_op jit(solution)/shard_map/reshape | solution.py:80
  31.9 0.0 reduce-scatter.2.cloned.1.call-update
  31.9 0.0 all-reduce.3.cloned.1.call-start
  32.0 62.4 %reduce-scatter.2.cloned.1.call-done = f32[16,512]{1,0:T(8,128)} async-done(((f32[128,512]{1,0:T(8,128)}), f32[16,512]{1,0:T(8,128)}) %reduce-scatter.2.cloned.1.call-update) | async-done | bytes 32784 | tf_op jit(solution)/shard_map/reduce_scatter | solution.py:79
  94.4 0.9 fusion.38
  95.3 2.5 %all-reduce = (f32[16]{0:T(128)S(1)}, f32[16]{0:T(128)S(1)}) all-reduce(f32[16]{0:T(128)S(1)} %get-tuple-element.20, f32[16]{0:T(128)S(1)} %get-tuple-element.19), channel_id=1, replica_groups=mesh['groups'=2,'events'=8,'heads'=2] {'heads'}, use_global_device_ids=true, to_apply=%region_4.5 | all-reduce | flops 32 | bytes 256 | tf_op jit(solution)/shard_map/psum | solution.py:87
  97.7 0.0 copy-done.3
  97.8 1.9 %fusion.26 = f32[16,1024]{1,0:T(8,128)} fusion(bf16[512,1024]{1,0:T(8,128)(2,1)S(1)} %copy-done, bf16[16,1024]{1,0:T(8,128)(2,1)S(1)} %copy-done.1, bf16[1024,1024]{1,0:T(8,128)(2,1)S(1)} %bitcast.32, f32[16,512]{1,0:T(8,128)} %reduce-scatter.2.cloned.1.call-done, f32[512]{0:T(512)S(1)} %copy-done.3, f32[16]{0:T(128)S(1)} %get-tuple-element.40, ...), kind=kOutput, calls=%fused_computation.27 | convolution fusion | flops 33644544 | bytes 2231296 | tf_op jit(solution)/shard_map/dot_general | solution.py:92
  99.6 0.0 all-reduce.3.cloned.1.call-update
  99.6 16.9 %all-reduce.3.cloned.1.call-done = f32[16,1024]{1,0:T(8,128)} async-done(((f32[16,1024]{1,0:T(8,128)}), f32[16,1024]{1,0:T(8,128)}) %all-reduce.3.cloned.1.call-update) | async-done | bytes 65552 | tf_op jit(solution)/shard_map/psum | solution.py:93
  116.6 1.5 %add_convert_fusion = bf16[16,1024]{1,0:T(8,128)(2,1)} fusion(f32[16,1024]{1,0:T(8,128)} %all-reduce.3.cloned.1.call-done, bf16[16,1024]{1,0:T(8,128)(2,1)S(1)} %copy-done.1), kind=kLoop, calls=%fused_computation.22 | loop fusion | flops 49152 | bytes 131072 | tf_op jit(solution)/shard_map/convert_element_type | solution.py:94
  (16 shorter events, 0.1 us)
Async XLA Ops:
  6.5 91.2 %copy-start = (bf16[512,1024]{1,0:T(8,128)(2,1)S(1)}, bf16[512,1024]{1,0:T(8,128)(2,1)}, u32[]{:S(2)}) copy-start(bf16[512,1024]{1,0:T(8,128)(2,1)} %param.17) | copy-start | bytes 3145732
  6.5 87.9 %reduce-scatter.2.cloned.1.call-start = ((), (), s32[]{:S(2)}) async-start(), calls=%async_computation.1 | async-start | bytes 294912 | tf_op jit(solution)/shard_map/reduce_scatter | solution.py:79
  6.5 7.8 %collective-permute-start = (bf16[1,16,1024]{2,1,0:T(8,128)(2,1)}, bf16[1,16,1024]{2,1,0:T(8,128)(2,1)S(1)}, u32[]{:S(2)}, u32[]{:S(2)}) collective-permute-start(bf16[1,16,1024]{2,1,0:T(8,128)(2,1)} %bitcast.35), channel_id=1, source_target_pairs={{0,2},{2,0},{4,6},{6,4},{8,10},{10,8},{12,14},{14,12},{1,3},{3,1},... | collective-permute-start | bytes 98312 | tf_op jit(solution)/shard_map/ppermute | solution.py:22
  12.2 2.2 %copy-start.1 = (bf16[16,1024]{1,0:T(8,128)(2,1)S(1)}, bf16[16,1024]{1,0:T(8,128)(2,1)}, u32[]{:S(2)}) copy-start(bf16[16,1024]{1,0:T(8,128)(2,1)} %param.9) | copy-start | bytes 98308
  12.2 9.3 %copy-start.2 = (s32[512]{0:T(512)S(1)}, s32[512]{0:T(512)}, u32[]{:S(2)}) copy-start(s32[512]{0:T(512)} %param.11) | copy-start | bytes 6148
  12.2 9.3 %copy-start.4 = (s32[128]{0:T(128)S(1)}, s32[128]{0:T(128)}, u32[]{:S(2)}) copy-start(s32[128]{0:T(128)} %param.10) | copy-start | bytes 1540
  14.4 4.3 %collective-permute-start.1 = (bf16[2,16,1024]{2,1,0:T(8,128)(2,1)S(1)}, bf16[2,16,1024]{2,1,0:T(8,128)(2,1)S(1)}, u32[]{:S(2)}, u32[]{:S(2)}) collective-permute-start(bf16[2,16,1024]{2,1,0:T(8,128)(2,1)S(1)} %pad_maximum_fusion.2), channel_id=1, source_target_pairs={{0,4},{2,6},{4,0},{6,2},{8,12},{10,14},{12,8},{14,10},{1,5},{3,7},... | collective-permute-start | bytes 196616 | tf_op jit(solution)/shard_map/ppermute | solution.py:22
  18.8 7.6 %collective-permute-start.2 = (bf16[4,16,1024]{2,1,0:T(8,128)(2,1)S(1)}, bf16[4,16,1024]{2,1,0:T(8,128)(2,1)S(1)}, u32[]{:S(2)}, u32[]{:S(2)}) collective-permute-start(bf16[4,16,1024]{2,1,0:T(8,128)(2,1)S(1)} %pad_maximum_fusion.1), channel_id=1, source_target_pairs={{0,8},{2,10},{4,12},{6,14},{8,0},{10,2},{12,4},{14,6},{1,9},{3,11}... | collective-permute-start | bytes 393224 | tf_op jit(solution)/shard_map/ppermute | solution.py:22
  27.5 70.3 %copy-start.3 = (f32[512]{0:T(512)S(1)}, f32[512]{0:T(512)}, u32[]{:S(2)}) copy-start(f32[512]{0:T(512)} %param.16) | copy-start | bytes 6148
  31.9 84.6 %all-reduce.3.cloned.1.call-start = ((), (), s32[]{:S(2)}) async-start(), calls=%async_computation.2 | async-start | bytes 131072 | tf_op jit(solution)/shard_map/psum | solution.py:93
Sparse Core Ops, SparseCore 0:
  32.0 62.3 reduce-scatter.1
  99.8 16.7 all-reduce.2
